TPU v7x, 512 devices: a whole 4x8x8 slice. The times are simulated.
512 devices in a mesh: gx: 32 (over z, y_hi, core), gy: 16 (over x, y_lo).
Axes of the slice: x: 4, y: 8 (y_hi: 2, y_lo: 4; y = y_hi * 4 + y_lo), z: 8, core: 2. Of those that a mesh axis runs over, the one named last changes fastest.
Arguments:
- design: float32 [256, 128, 128], P('gx', 'gy'), may hold values from 0.06 to 0.9
- passive: int32 [256, 128, 128], P('gx', 'gy'), may hold values 0 or 1
- basis_pairs: float32 [4, 2, 3, 256, 128, 128], P(None, None, None, 'gx', 'gy'), may hold values from -6 to 6
- supports: int32 [256, 128, 128], P('gx', 'gy'), may hold values 0 or 1
- stiffness: float32 [24, 24], replicated, may hold values from -1.25 to 1.25
- mass_matrix: float32 [24, 24], replicated, may hold values from -1.25 to 1.25
- volume_fraction: float32 [64], replicated, may hold values from 0.26 to 0.36
Outputs:
- sensitivity: float32 [256, 128, 128], P('gx', 'gy')
- design_next: float32 [256, 128, 128], P('gx', 'gy')
All inputs are finite; a program needn't handle non-finite values. No bound on the sum of `passive` or of `supports` on one device may be relied on, other than what follows from the above.
Results may differ from a plain program's by a relative error of at most 0.0003.
Values sent between devices are 32-bit elements; how exact they have to be, the bound alone decides.
No kernel may reach another device: no remote copies, remote signals or barrier semaphores. Data moves between devices by JAX's collectives and lax.ppermute only.
A program may use at most 64 MiB of HBM per device.

v0:
```python
import math
import jax
import jax.numpy as jnp
from jax import lax
from jax.sharding import PartitionSpec as P

BISECT = 6
REGIONS = 64
PENALTY_SCALE = 3.0 * (1.0 - 0.001)
OMEGA_SQUARED = 0.5
MOVE_LIMIT = 0.2


def with_halo(cells, sides, width):
    for axis, dim in sides:
        count = lax.axis_size(axis)
        ends = count - 1
        head = lax.slice_in_dim(cells, 0, width, axis=dim)
        tail = lax.slice_in_dim(cells, cells.shape[dim] - width, cells.shape[dim], axis=dim)
        cells = jnp.concatenate(
            [
                lax.ppermute(tail, axis, [(i, (i + 1) % count) for i in range(ends)]),
                cells,
                lax.ppermute(head, axis, [((i + 1) % count, i) for i in range(ends)]),
            ],
            axis=dim,
        )
    return cells


def from_behind(value, axis, steps):
    count = lax.axis_size(axis)
    initial, last = (max(0, -steps), min(count, count - steps))
    return lax.ppermute(value, axis, [(source, source + steps) for source in range(initial, last)])


def filter_taps():
    tap_list = []
    for offset_x in range(-2, 3):
        for offset_y in range(-2, 3):
            for offset_z in range(-2, 3):
                weight = 3.0 - math.sqrt(
                    offset_x * offset_x + offset_y * offset_y + offset_z * offset_z
                )
                if weight > 0.0:
                    tap_list.append((offset_x, offset_y, offset_z, weight))
    return tap_list


def stencil(padded, block_shape):
    result = jnp.zeros(block_shape, jnp.float32)
    for offset_x, offset_y, offset_z, weight in filter_taps():
        result = (
            result
            + weight
            * padded[
                2 + offset_x : 2 + offset_x + block_shape[0],
                2 + offset_y : 2 + offset_y + block_shape[1],
                2 + offset_z : 2 + offset_z + block_shape[2],
            ]
        )
    return result


def element_terms(extended, stiffness, mass_matrix):
    pair_count = extended.shape[0]
    cells_x = extended.shape[3] - 1
    cells_y = extended.shape[4] - 1
    cells_z = extended.shape[5] - 1
    stiff_energy = jnp.zeros((cells_x * cells_y * cells_z,), jnp.float32)
    mass_energy = jnp.zeros((cells_x * cells_y * cells_z,), jnp.float32)
    for pair_index in range(pair_count):
        vectors = []
        for member in range(2):
            row_list = []
            for corner_x in (0, 1):
                for corner_y in (0, 1):
                    for corner_z in (0, 1):
                        for component in range(3):
                            row_list.append(
                                extended[
                                    pair_index,
                                    member,
                                    component,
                                    corner_x : corner_x + cells_x,
                                    corner_y : corner_y + cells_y,
                                    corner_z : corner_z + cells_z,
                                ].reshape(-1)
                            )
            vectors.append(jnp.stack(row_list))
        state_rows, adjoint_rows = vectors
        stiff_energy = stiff_energy + jnp.sum(
            state_rows * jnp.dot(stiffness, adjoint_rows, precision=lax.Precision.HIGHEST), axis=0
        )
        mass_energy = mass_energy + jnp.sum(
            state_rows * jnp.dot(mass_matrix, adjoint_rows, precision=lax.Precision.HIGHEST), axis=0
        )
    return (
        stiff_energy.reshape(cells_x, cells_y, cells_z),
        mass_energy.reshape(cells_x, cells_y, cells_z),
    )


def shards(design, passive, basis_pairs, supports, stiffness, mass_matrix, volume_fraction):
    block_shape = design.shape
    size_x, size_y, size_z = block_shape
    devices_x = lax.axis_size("gx")
    devices_y = lax.axis_size("gy")
    index_x = lax.axis_index("gx")
    index_y = lax.axis_index("gy")
    grid_x = size_x * devices_x
    grid_y = size_y * devices_y
    spread_x = jnp.arange(size_x + 4, dtype=jnp.int32) + index_x * size_x - 2
    spread_y = jnp.arange(size_y + 4, dtype=jnp.int32) + index_y * size_y - 2
    valid_x = ((spread_x >= 0) & (spread_x < grid_x)).astype(jnp.float32)
    valid_y = ((spread_y >= 0) & (spread_y < grid_y)).astype(jnp.float32)
    valid_z = jnp.pad(jnp.ones((size_z,), jnp.float32), 2)
    inside = valid_x[:, None, None] * valid_y[None, :, None] * valid_z[None, None, :]
    weight_sum = stencil(inside, block_shape)
    design_wide = with_halo(design, (("gx", 0), ("gy", 1)), 2)
    design_wide = jnp.pad(design_wide, ((0, 0), (0, 0), (2, 2)))
    physical = jnp.where(passive == 1, 1.0, stencil(design_wide, block_shape) / weight_sum)
    fields = basis_pairs * (1 - supports).astype(jnp.float32)
    rim_first = from_behind(fields[:, :, :, :1], "gx", -1)
    widened = jnp.concatenate([fields, rim_first], axis=3)
    rim_second = from_behind(widened[:, :, :, :, :1], "gy", -1)
    extended = jnp.concatenate([widened, rim_second], axis=4)
    extended = jnp.pad(extended, ((0, 0), (0, 0), (0, 0), (0, 0), (0, 0), (0, 1)))
    stiff_energy, mass_energy = element_terms(extended, stiffness, mass_matrix)
    raw_sensitivity = -(
        PENALTY_SCALE * physical * physical * stiff_energy - OMEGA_SQUARED * mass_energy
    )
    raw_sensitivity = jnp.where(passive == 1, 0.0, raw_sensitivity)
    scaled_wide = with_halo(raw_sensitivity / weight_sum, (("gx", 0), ("gy", 1)), 2)
    scaled_wide = jnp.pad(scaled_wide, ((0, 0), (0, 0), (2, 2)))
    sensitivity = stencil(scaled_wide, block_shape)
    benefit = jnp.maximum(-sensitivity, 0.0)
    floor_value = jnp.maximum(design - MOVE_LIMIT, 0.0)
    ceiling = jnp.minimum(design + MOVE_LIMIT, 1.0)
    band_cells = size_z // REGIONS
    target = volume_fraction * float(grid_x * grid_y * band_cells)

    def candidate(multiplier):
        per_cell = jnp.repeat(multiplier, band_cells)[None, None, :]
        trial = design * jnp.sqrt(benefit / per_cell)
        return jnp.where(passive == 1, 1.0, jnp.minimum(ceiling, jnp.maximum(floor_value, trial)))

    def region_sum(field):
        return jnp.sum(field, axis=(0, 1)).reshape(REGIONS, band_cells).sum(axis=1)

    levels = BISECT

    def bisect_round(round_index, bracket):
        low_end, high_end = bracket
        level_nodes = [(low_end, high_end)]
        midpoints = []
        for depth in range(levels):
            next_nodes = []
            for node_low, node_high in level_nodes:
                middle = jnp.sqrt(node_low * node_high)
                midpoints.append(middle)
                next_nodes.append((node_low, middle))
                next_nodes.append((middle, node_high))
            level_nodes = next_nodes
        trial_multipliers = jnp.stack(midpoints)
        per_cell = jnp.repeat(trial_multipliers, band_cells, axis=1)[:, None, None, :]
        trial = design[None] * jnp.sqrt(benefit[None] / per_cell)
        fields_of = jnp.where(
            passive[None] == 1,
            1.0,
            jnp.minimum(ceiling[None], jnp.maximum(floor_value[None], trial)),
        )
        partial_volumes = (
            jnp.sum(fields_of, axis=(1, 2)).reshape(len(midpoints), REGIONS, band_cells).sum(axis=2)
        )
        volumes = lax.psum(partial_volumes, ("gx", "gy"))
        position = jnp.zeros((REGIONS,), jnp.int32)
        for depth in range(levels):
            middle = jnp.sqrt(low_end * high_end)
            heap_index = position + (2**depth - 1)
            chosen = jnp.take_along_axis(volumes, heap_index[None, :], axis=0)[0]
            heavier = chosen > target
            low_end = jnp.where(heavier, middle, low_end)
            high_end = jnp.where(heavier, high_end, middle)
            position = 2 * position + heavier.astype(jnp.int32)
        return (low_end, high_end)

    start = (jnp.full((REGIONS,), 0.0001, jnp.float32), jnp.full((REGIONS,), 10000.0, jnp.float32))
    low_end, high_end = bisect_round(0, start)
    design_next = candidate(jnp.sqrt(low_end * high_end))
    return (sensitivity, design_next)


def solution(mesh):
    placed = (
        P("gx", "gy", None),
        P("gx", "gy", None),
        P(None, None, None, "gx", "gy", None),
        P("gx", "gy", None),
        P(),
        P(),
        P(),
    )
    return jax.shard_map(
        shards,
        mesh=mesh,
        in_specs=placed,
        out_specs=(P("gx", "gy", None), P("gx", "gy", None)),
        check_vma=False,
    )
```

profile of v0, /device:TPU:1, one launch (start us, length us, event | category | flops | bytes accessed | tf_op | source)
XLA Modules:
  0.0 233.9 jit_solution(4660837941216454200)
XLA Ops:
  1.4 8.8 %collective-permute-start.1 = (f32[2,8,128]{2,1,0:T(8,128)S(1)}, f32[2,8,128]{2,1,0:T(8,128)S(1)}, u32[]{:S(2)}, u32[]{:S(2)}) collective-permute-start(f32[2,8,128]{2,1,0:T(8,128)S(1)} %get-tuple-element.214), channel_id=1, source_target_pairs={{16,0},{32,16},{48,32},{64,48},{80,64},{96,80},{112,96},{128,112},... | collective-permute-start | bytes 24584 | tf_op jit(solution)/shard_map/ppermute | solution.py:24
  10.2 2.0 collective-permute-start
  13.0 1.2 broadcast_multiply_fusion
  14.2 2.3 %collective-permute-start.4 = (f32[4,2,3,1,8,128]{5,4,3,2,1,0:T(8,128)S(1)}, f32[4,2,3,1,8,128]{5,4,3,2,1,0:T(8,128)S(1)}, u32[]{:S(2)}, u32[]{:S(2)}) collective-permute-start(f32[4,2,3,1,8,128]{5,4,3,2,1,0:T(8,128)S(1)} %slice.2424), channel_id=1, source_target_pairs={{16,0},{32,16},{48,32},{64,48},{80,64},{96,80},{112,96},{128,112},... | collective-permute-start | bytes 294920 | tf_op jit(solution)/shard_map/ppermute | solution.py:34
  18.3 2.3 collective-permute-start.2
  20.6 1.3 collective-permute-start.3
  22.4 2.7 %collective-permute-done.3 = f32[12,2,128]{2,1,0:T(2,128)S(1)} collective-permute-done((f32[12,2,128]{2,1,0:T(2,128)S(1)}, f32[12,2,128]{2,1,0:T(2,128)S(1)}, u32[]{:S(2)}, u32[]{:S(2)}) %collective-permute-start.3) | collective-permute-done | bytes 12320 | tf_op jit(solution)/shard_map/ppermute | solution.py:24
  25.4 1.3 collective-permute-start.5
  29.0 4.9 %collective-permute-done.5 = f32[4,2,3,9,1,128]{5,3,4,2,1,0:T(8,128)S(1)} collective-permute-done((f32[4,2,3,9,1,128]{5,3,4,2,1,0:T(8,128)S(1)}, f32[4,2,3,9,1,128]{5,3,4,2,1,0:T(8,128)S(1)}, u32[]{:S(2)}, u32[]{:S(2)}) %collective-permute-start.5) | collective-permute-done | bytes 110624 | tf_op jit(solution)/shard_map/ppermute | solution.py:34
  35.1 1.0 pad_slice_fusion.79
  36.1 1.1 pad_slice_fusion.48
  38.0 1.1 fusion.373
  40.0 3.7 %stack.24 = f32[24,8192]{1,0:T(8,128)S(1)} concatenate(f32[1,8192]{1,0:T(1,128)} %bitcast.576, f32[1,8192]{1,0:T(1,128)} %bitcast.575, f32[1,8192]{1,0:T(1,128)} %bitcast.574, f32[1,8192]{1,0:T(1,128)} %bitcast.624, f32[1,8192]{1,0:T(1,128)} %bitcast.497, f32[1,8192]{1,0:T(1,128)} %bitcast.498, f32[1,8192]{1,0:T(1,128)} %bitcast.623, f32[1,8192]{1,0:T(1,128)} %bitcast.622, ...), dimensions={0} | concatenate | bytes 1572864 | tf_op jit(solution)/shard_map/stack | solution.py:90
  43.8 5.8 %stack.25 = f32[24,8192]{1,0:T(8,128)} concatenate(f32[1,8192]{1,0:T(1,128)} %bitcast.571, f32[1,8192]{1,0:T(1,128)} %bitcast.570, f32[1,8192]{1,0:T(1,128)} %bitcast.588, f32[1,8192]{1,0:T(1,128)} %bitcast.468, f32[1,8192]{1,0:T(1,128)} %bitcast.469, f32[1,8192]{1,0:T(1,128)} %bitcast.470, f32[1,8192]{1,0:T(1,128)} %bitcast.617, f32[1,8192]{1,0:T(1,128)} %bitcast.616, ...), dimensions={0} | concatenate | bytes 1572864 | tf_op jit(solution)/shard_map/stack | solution.py:90
  49.6 2.7 %fusion.17 = f32[8192]{0:T(1024)} fusion(f32[24,8192]{1,0:T(8,128)S(1)} %stack.24, f32[24,8192]{1,0:T(8,128)} %stack.25, f32[24,24]{1,0:T(8,128)S(1)} %copy-done), kind=kOutput, calls=%fused_computation.153 | convolution fusion | flops 57008128 | bytes 1607936 | tf_op jit(solution)/shard_map/dot_general | solution.py:96
  52.3 1.5 fusion.13
  53.8 3.7 %stack.31 = f32[24,8192]{1,0:T(8,128)S(1)} concatenate(f32[1,8192]{1,0:T(1,128)} %bitcast.564, f32[1,8192]{1,0:T(1,128)} %bitcast.584, f32[1,8192]{1,0:T(1,128)} %bitcast.580, f32[1,8192]{1,0:T(1,128)} %bitcast.514, f32[1,8192]{1,0:T(1,128)} %bitcast.515, f32[1,8192]{1,0:T(1,128)} %bitcast.516, f32[1,8192]{1,0:T(1,128)} %bitcast.531, f32[1,8192]{1,0:T(1,128)} %bitcast.530, ...), dimensions={0} | concatenate | bytes 1572864 | tf_op jit(solution)/shard_map/stack | solution.py:90
  57.5 5.8 %stack.30 = f32[24,8192]{1,0:T(8,128)} concatenate(f32[1,8192]{1,0:T(1,128)} %bitcast.558, f32[1,8192]{1,0:T(1,128)} %bitcast.557, f32[1,8192]{1,0:T(1,128)} %bitcast.556, f32[1,8192]{1,0:T(1,128)} %bitcast.466, f32[1,8192]{1,0:T(1,128)} %bitcast.479, f32[1,8192]{1,0:T(1,128)} %bitcast.480, f32[1,8192]{1,0:T(1,128)} %bitcast.513, f32[1,8192]{1,0:T(1,128)} %bitcast.512, ...), dimensions={0} | concatenate | bytes 1572864 | tf_op jit(solution)/shard_map/stack | solution.py:90
  63.3 2.7 %fusion.20 = f32[8192]{0:T(1024)} fusion(f32[24,8192]{1,0:T(8,128)} %stack.30, f32[24,8192]{1,0:T(8,128)S(1)} %stack.31, f32[24,24]{1,0:T(8,128)S(1)} %copy-done), kind=kOutput, calls=%fused_computation.156 | convolution fusion | flops 57008128 | bytes 1607936 | tf_op jit(solution)/shard_map/dot_general | solution.py:96
  66.0 1.5 fusion.16
  69.5 3.7 %stack.27 = f32[24,8192]{1,0:T(8,128)S(1)} concatenate(f32[1,8192]{1,0:T(1,128)} %bitcast.569, f32[1,8192]{1,0:T(1,128)} %bitcast.568, f32[1,8192]{1,0:T(1,128)} %bitcast.567, f32[1,8192]{1,0:T(1,128)} %bitcast.534, f32[1,8192]{1,0:T(1,128)} %bitcast.535, f32[1,8192]{1,0:T(1,128)} %bitcast.536, f32[1,8192]{1,0:T(1,128)} %bitcast.610, f32[1,8192]{1,0:T(1,128)} %bitcast.609, ...), dimensions={0} | concatenate | bytes 1572864 | tf_op jit(solution)/shard_map/stack | solution.py:90
  73.3 3.6 %stack.26 = f32[24,8192]{1,0:T(8,128)S(1)} concatenate(f32[1,8192]{1,0:T(1,128)S(1)} %bitcast.563, f32[1,8192]{1,0:T(1,128)S(1)} %bitcast.562, f32[1,8192]{1,0:T(1,128)S(1)} %bitcast.561, f32[1,8192]{1,0:T(1,128)S(1)} %bitcast.450, f32[1,8192]{1,0:T(1,128)S(1)} %bitcast.451, f32[1,8192]{1,0:T(1,128)S(1)} %bitcast.452, f32[1,8192]{1,0:T(1,128)} %bitcast.611, f32[1,8192]{1,0:T(1,128)} %bitcast.607, ...), dimensions={0} | concatenate | bytes 1572864 | tf_op jit(solution)/shard_map/stack | solution.py:90
  79.0 3.4 %stack.29 = f32[24,8192]{1,0:T(8,128)S(1)} concatenate(f32[1,8192]{1,0:T(1,128)S(1)} %bitcast.549, f32[1,8192]{1,0:T(1,128)S(1)} %bitcast.548, f32[1,8192]{1,0:T(1,128)S(1)} %bitcast.547, f32[1,8192]{1,0:T(1,128)S(1)} %bitcast.438, f32[1,8192]{1,0:T(1,128)S(1)} %bitcast.439, f32[1,8192]{1,0:T(1,128)S(1)} %bitcast.440, f32[1,8192]{1,0:T(1,128)} %bitcast.602, f32[1,8192]{1,0:T(1,128)} %bitcast.601, ...), dimensions={0} | concatenate | bytes 1572864 | tf_op jit(solution)/shard_map/stack | solution.py:90
  82.5 1.2 stack.28
  85.5 1.2 fusion.98
  86.8 8.2 %collective-permute-start.6 = (f32[2,8,128]{2,1,0:T(8,128)S(1)}, f32[2,8,128]{2,1,0:T(8,128)S(1)}, u32[]{:S(2)}, u32[]{:S(2)}) collective-permute-start(f32[2,8,128]{2,1,0:T(8,128)S(1)} %get-tuple-element.212), channel_id=1, source_target_pairs={{0,16},{16,32},{32,48},{48,64},{64,80},{80,96},{96,112},{112,128},... | collective-permute-start | bytes 24584 | tf_op jit(solution)/shard_map/ppermute | solution.py:22
  94.9 1.9 collective-permute-start.7
  96.9 6.9 %collective-permute-done.7 = f32[2,8,128]{2,1,0:T(8,128)S(1)} collective-permute-done((f32[2,8,128]{2,1,0:T(8,128)S(1)}, f32[2,8,128]{2,1,0:T(8,128)S(1)}, u32[]{:S(2)}, u32[]{:S(2)}) %collective-permute-start.7) | collective-permute-done | bytes 8224 | tf_op jit(solution)/shard_map/ppermute | solution.py:24
  103.8 3.1 %collective-permute-start.8 = (f32[12,2,128]{2,1,0:T(2,128)S(1)}, f32[12,2,128]{2,1,0:T(2,128)S(1)}, u32[]{:S(2)}, u32[]{:S(2)}) collective-permute-start(f32[12,2,128]{2,1,0:T(2,128)S(1)} %get-tuple-element.203), channel_id=1, source_target_pairs={{0,1},{1,2},{2,3},{3,4},{4,5},{5,6},{6,7},{7,8},{8,9},{9,10},{10,1... | collective-permute-start | bytes 36872 | tf_op jit(solution)/shard_map/ppermute | solution.py:22
  106.9 1.3 collective-permute-start.9
  108.4 5.7 %collective-permute-done.9 = f32[12,2,128]{2,1,0:T(2,128)S(1)} collective-permute-done((f32[12,2,128]{2,1,0:T(2,128)S(1)}, f32[12,2,128]{2,1,0:T(2,128)S(1)}, u32[]{:S(2)}, u32[]{:S(2)}) %collective-permute-start.9) | collective-permute-done | bytes 12320 | tf_op jit(solution)/shard_map/ppermute | solution.py:24
  116.1 111.8 %psum.7 = f32[63,64]{1,0:T(8,128)S(1)} all-reduce(f32[63,64]{1,0:T(8,128)S(1)} %copy.118), channel_id=1, replica_groups=mesh['gx'=32,'gy'=16] {'gx','gy'}, use_global_device_ids=true, to_apply=%region_10.11 | all-reduce | flops 4032 | bytes 32256 | tf_op jit(solution)/shard_map/psum | solution.py:176
  (198 shorter events, 22.7 us)
Async XLA Ops:
  0.6 49.0 %copy-start = (f32[24,24]{1,0:T(8,128)S(1)}, f32[24,24]{1,0:T(8,128)}, u32[]{:S(2)}) copy-start(f32[24,24]{1,0:T(8,128)} %param.14) | copy-start | bytes 6916
  0.6 17.0 %copy-start.3 = (f32[8,8,128]{2,1,0:T(8,128)S(1)}, f32[8,8,128]{2,1,0:T(8,128)}, u32[]{:S(2)}) copy-start(f32[8,8,128]{2,1,0:T(8,128)} %param.9) | copy-start | bytes 98308
  1.4 16.8 %collective-permute-start.1 = (f32[2,8,128]{2,1,0:T(8,128)S(1)}, f32[2,8,128]{2,1,0:T(8,128)S(1)}, u32[]{:S(2)}, u32[]{:S(2)}) collective-permute-start(f32[2,8,128]{2,1,0:T(8,128)S(1)} %get-tuple-element.214), channel_id=1, source_target_pairs={{16,0},{32,16},{48,32},{64,48},{80,64},{96,80},{112,96},{128,112},... | collective-permute-start | bytes 24584 | tf_op jit(solution)/shard_map/ppermute | solution.py:24
  10.2 7.4 %collective-permute-start = (f32[2,8,128]{2,1,0:T(8,128)S(1)}, f32[2,8,128]{2,1,0:T(8,128)S(1)}, u32[]{:S(2)}, u32[]{:S(2)}) collective-permute-start(f32[2,8,128]{2,1,0:T(8,128)S(1)} %get-tuple-element.215), channel_id=1, source_target_pairs={{0,16},{16,32},{32,48},{48,64},{64,80},{80,96},{96,112},{112,128},... | collective-permute-start | bytes 24584 | tf_op jit(solution)/shard_map/ppermute | solution.py:22
  14.2 11.1 %collective-permute-start.4 = (f32[4,2,3,1,8,128]{5,4,3,2,1,0:T(8,128)S(1)}, f32[4,2,3,1,8,128]{5,4,3,2,1,0:T(8,128)S(1)}, u32[]{:S(2)}, u32[]{:S(2)}) collective-permute-start(f32[4,2,3,1,8,128]{5,4,3,2,1,0:T(8,128)S(1)} %slice.2424), channel_id=1, source_target_pairs={{16,0},{32,16},{48,32},{64,48},{80,64},{96,80},{112,96},{128,112},... | collective-permute-start | bytes 294920 | tf_op jit(solution)/shard_map/ppermute | solution.py:34
  18.3 4.1 %collective-permute-start.2 = (f32[12,2,128]{2,1,0:T(2,128)S(1)}, f32[12,2,128]{2,1,0:T(2,128)S(1)}, u32[]{:S(2)}, u32[]{:S(2)}) collective-permute-start(f32[12,2,128]{2,1,0:T(2,128)S(1)} %get-tuple-element.205), channel_id=1, source_target_pairs={{0,1},{1,2},{2,3},{3,4},{4,5},{5,6},{6,7},{7,8},{8,9},{9,10},{10,1... | collective-permute-start | bytes 36872 | tf_op jit(solution)/shard_map/ppermute | solution.py:22
  20.6 4.6 %collective-permute-start.3 = (f32[12,2,128]{2,1,0:T(2,128)S(1)}, f32[12,2,128]{2,1,0:T(2,128)S(1)}, u32[]{:S(2)}, u32[]{:S(2)}) collective-permute-start(f32[12,2,128]{2,1,0:T(2,128)S(1)} %get-tuple-element.206), channel_id=1, source_target_pairs={{1,0},{2,1},{3,2},{4,3},{5,4},{6,5},{7,6},{8,7},{9,8},{10,9},{11,1... | collective-permute-start | bytes 36872 | tf_op jit(solution)/shard_map/ppermute | solution.py:24
  25.4 8.5 %collective-permute-start.5 = (f32[4,2,3,9,1,128]{5,3,4,2,1,0:T(8,128)S(1)}, f32[4,2,3,9,1,128]{5,3,4,2,1,0:T(8,128)S(1)}, u32[]{:S(2)}, u32[]{:S(2)}) collective-permute-start(f32[4,2,3,9,1,128]{5,3,4,2,1,0:T(8,128)S(1)} %copy.114), channel_id=1, source_target_pairs={{1,0},{2,1},{3,2},{4,3},{5,4},{6,5},{7,6},{8,7},{9,8},{10,9},{11,1... | collective-permute-start | bytes 331784 | tf_op jit(solution)/shard_map/ppermute | solution.py:34
  43.8 8.5 %copy-start.4 = (f32[24,24]{1,0:T(8,128)S(1)}, f32[24,24]{1,0:T(8,128)}, u32[]{:S(2)}) copy-start(f32[24,24]{1,0:T(8,128)} %param.13) | copy-start | bytes 6916
  68.3 4.8 %copy-start.10 = (f32[1,1,1,8,8,128]{5,4,3,2,1,0:T(8,128)S(1)}, f32[1,1,1,8,8,128]{5,4,3,2,1,0:T(8,128)}, u32[]{:S(2)}) copy-start(f32[1,1,1,8,8,128]{5,4,3,2,1,0:T(8,128)} %get-tuple-element.17) | copy-start | bytes 98308
  68.3 4.8 %copy-start.11 = (f32[1,1,1,8,8,128]{5,4,3,2,1,0:T(8,128)S(1)}, f32[1,1,1,8,8,128]{5,4,3,2,1,0:T(8,128)}, u32[]{:S(2)}) copy-start(f32[1,1,1,8,8,128]{5,4,3,2,1,0:T(8,128)} %get-tuple-element.18) | copy-start | bytes 98308
  68.3 4.8 %copy-start.12 = (f32[1,1,1,8,8,128]{5,4,3,2,1,0:T(8,128)S(1)}, f32[1,1,1,8,8,128]{5,4,3,2,1,0:T(8,128)}, u32[]{:S(2)}) copy-start(f32[1,1,1,8,8,128]{5,4,3,2,1,0:T(8,128)} %get-tuple-element.19) | copy-start | bytes 98308
  68.3 4.8 %copy-start.13 = (f32[1,1,1,8,8,128]{5,4,3,2,1,0:T(8,128)S(1)}, f32[1,1,1,8,8,128]{5,4,3,2,1,0:T(8,128)}, u32[]{:S(2)}) copy-start(f32[1,1,1,8,8,128]{5,4,3,2,1,0:T(8,128)} %get-tuple-element.20) | copy-start | bytes 98308
  68.4 4.8 %copy-start.14 = (f32[1,1,1,8,8,128]{5,4,3,2,1,0:T(8,128)S(1)}, f32[1,1,1,8,8,128]{5,4,3,2,1,0:T(8,128)}, u32[]{:S(2)}) copy-start(f32[1,1,1,8,8,128]{5,4,3,2,1,0:T(8,128)} %get-tuple-element.21) | copy-start | bytes 98308
  68.4 4.8 %copy-start.15 = (f32[1,1,1,8,8,128]{5,4,3,2,1,0:T(8,128)S(1)}, f32[1,1,1,8,8,128]{5,4,3,2,1,0:T(8,128)}, u32[]{:S(2)}) copy-start(f32[1,1,1,8,8,128]{5,4,3,2,1,0:T(8,128)} %get-tuple-element.22) | copy-start | bytes 98308
  68.4 4.8 %copy-start.16 = (f32[1,1,1,8,8,128]{5,4,3,2,1,0:T(8,128)S(1)}, f32[1,1,1,8,8,128]{5,4,3,2,1,0:T(8,128)}, u32[]{:S(2)}) copy-start(f32[1,1,1,8,8,128]{5,4,3,2,1,0:T(8,128)} %get-tuple-element.23) | copy-start | bytes 98308
  68.4 4.8 %copy-start.17 = (f32[1,1,1,8,8,128]{5,4,3,2,1,0:T(8,128)S(1)}, f32[1,1,1,8,8,128]{5,4,3,2,1,0:T(8,128)}, u32[]{:S(2)}) copy-start(f32[1,1,1,8,8,128]{5,4,3,2,1,0:T(8,128)} %get-tuple-element.24) | copy-start | bytes 98308
  68.4 4.8 %copy-start.18 = (f32[1,1,1,8,8,128]{5,4,3,2,1,0:T(8,128)S(1)}, f32[1,1,1,8,8,128]{5,4,3,2,1,0:T(8,128)}, u32[]{:S(2)}) copy-start(f32[1,1,1,8,8,128]{5,4,3,2,1,0:T(8,128)} %get-tuple-element.25) | copy-start | bytes 98308
  68.4 4.8 %copy-start.19 = (f32[1,1,1,8,8,128]{5,4,3,2,1,0:T(8,128)S(1)}, f32[1,1,1,8,8,128]{5,4,3,2,1,0:T(8,128)}, u32[]{:S(2)}) copy-start(f32[1,1,1,8,8,128]{5,4,3,2,1,0:T(8,128)} %get-tuple-element.26) | copy-start | bytes 98308
  68.4 4.8 %copy-start.20 = (f32[1,1,1,8,8,128]{5,4,3,2,1,0:T(8,128)S(1)}, f32[1,1,1,8,8,128]{5,4,3,2,1,0:T(8,128)}, u32[]{:S(2)}) copy-start(f32[1,1,1,8,8,128]{5,4,3,2,1,0:T(8,128)} %get-tuple-element.27) | copy-start | bytes 98308
  77.9 4.5 %copy-start.31 = (f32[1,1,1,8,8,128]{5,4,3,2,1,0:T(8,128)S(1)}, f32[1,1,1,8,8,128]{5,4,3,2,1,0:T(8,128)}, u32[]{:S(2)}) copy-start(f32[1,1,1,8,8,128]{5,4,3,2,1,0:T(8,128)} %get-tuple-element.194) | copy-start | bytes 98308
  77.9 4.5 %copy-start.32 = (f32[1,1,1,8,8,128]{5,4,3,2,1,0:T(8,128)S(1)}, f32[1,1,1,8,8,128]{5,4,3,2,1,0:T(8,128)}, u32[]{:S(2)}) copy-start(f32[1,1,1,8,8,128]{5,4,3,2,1,0:T(8,128)} %get-tuple-element.195) | copy-start | bytes 98308
  85.5 11.4 %copy-start.60 = (s32[1,64,1]{1,2,0:T(1,128)S(1)}, s32[1,64,1]{1,2,0:T(1,128)}, u32[]{:S(2)}) copy-start(s32[1,64,1]{1,2,0:T(1,128)} %broadcast_bitcast_fusion) | copy-start | bytes 772
  85.5 22.7 %copy-start.56 = (f32[63,64]{0,1:T(8,128)S(1)}, f32[63,64]{0,1:T(8,128)}, u32[]{:S(2)}) copy-start(f32[63,64]{0,1:T(8,128)} %constant.25.clone.1) | copy-start | bytes 48388
  86.8 10.1 %collective-permute-start.6 = (f32[2,8,128]{2,1,0:T(8,128)S(1)}, f32[2,8,128]{2,1,0:T(8,128)S(1)}, u32[]{:S(2)}, u32[]{:S(2)}) collective-permute-start(f32[2,8,128]{2,1,0:T(8,128)S(1)} %get-tuple-element.212), channel_id=1, source_target_pairs={{0,16},{16,32},{32,48},{48,64},{64,80},{80,96},{96,112},{112,128},... | collective-permute-start | bytes 24584 | tf_op jit(solution)/shard_map/ppermute | solution.py:22
  94.9 8.9 %collective-permute-start.7 = (f32[2,8,128]{2,1,0:T(8,128)S(1)}, f32[2,8,128]{2,1,0:T(8,128)S(1)}, u32[]{:S(2)}, u32[]{:S(2)}) collective-permute-start(f32[2,8,128]{2,1,0:T(8,128)S(1)} %get-tuple-element.213), channel_id=1, source_target_pairs={{16,0},{32,16},{48,32},{64,48},{80,64},{96,80},{112,96},{128,112},... | collective-permute-start | bytes 24584 | tf_op jit(solution)/shard_map/ppermute | solution.py:24
  103.8 4.6 %collective-permute-start.8 = (f32[12,2,128]{2,1,0:T(2,128)S(1)}, f32[12,2,128]{2,1,0:T(2,128)S(1)}, u32[]{:S(2)}, u32[]{:S(2)}) collective-permute-start(f32[12,2,128]{2,1,0:T(2,128)S(1)} %get-tuple-element.203), channel_id=1, source_target_pairs={{0,1},{1,2},{2,3},{3,4},{4,5},{5,6},{6,7},{7,8},{8,9},{9,10},{10,1... | collective-permute-start | bytes 36872 | tf_op jit(solution)/shard_map/ppermute | solution.py:22
  106.9 7.1 %collective-permute-start.9 = (f32[12,2,128]{2,1,0:T(2,128)S(1)}, f32[12,2,128]{2,1,0:T(2,128)S(1)}, u32[]{:S(2)}, u32[]{:S(2)}) collective-permute-start(f32[12,2,128]{2,1,0:T(2,128)S(1)} %get-tuple-element.204), channel_id=1, source_target_pairs={{1,0},{2,1},{3,2},{4,3},{5,4},{6,5},{7,6},{8,7},{9,8},{10,9},{11,1... | collective-permute-start | bytes 36872 | tf_op jit(solution)/shard_map/ppermute | solution.py:24
  108.4 6.5 %copy-start.57 = (f32[8,8,128]{2,1,0:T(8,128)S(1)}, f32[8,8,128]{2,1,0:T(8,128)}, u32[]{:S(2)}) copy-start(f32[8,8,128]{2,1,0:T(8,128)} %get-tuple-element.207) | copy-start | bytes 98308
  108.4 6.5 %copy-start.58 = (f32[8,8,128]{2,1,0:T(8,128)S(1)}, f32[8,8,128]{2,1,0:T(8,128)}, u32[]{:S(2)}) copy-start(f32[8,8,128]{2,1,0:T(8,128)} %get-tuple-element.208) | copy-start | bytes 98308
  114.3 114.4 %copy-start.59 = (f32[64]{0:T(128)S(1)}, f32[64]{0:T(128)}, u32[]{:S(2)}) copy-start(f32[64]{0:T(128)} %param.15) | copy-start | bytes 772
  114.8 118.4 %copy-start.30 = (f32[8,8,128]{2,1,0:T(8,128)}, f32[8,8,128]{2,1,0:T(8,128)S(1)}, u32[]{:S(2)}) copy-start(f32[8,8,128]{2,1,0:T(8,128)S(1)} %get-tuple-element.6) | copy-start | bytes 98308
  (39 other events, 111.5 us)
where the time goes:
time: 236 us; the launch traced here: 234 us
  blocking collectives  112 us (47%)
  local copies, waits for them, and re-layouts  46.5 us (20%)
  starting transfers between devices  32.5 us (14%)
  waiting for transfers between devices  20.3 us (9%)
  matrix products  11.7 us (5%)
  other arithmetic  9.3 us (4%)
    psum x1, blocking collectives, bisect_round(): volumes = lax.psum(partial_volumes, ('gx', 'gy'))  112 us
    another operation x8, local copies, waits for them, and re-layouts, element_terms(): vectors.append(jnp.stack(row_list))  31 us
    ppermute x4, starting transfers between devices, with_halo(): lax.ppermute(tail, axis, [(i, (i + 1) % count) for i in range(ends)])  15.6 us
    ppermute x4, waiting for transfers between devices, with_halo(): lax.ppermute(head, axis, [((i + 1) % count, i) for i in range(ends)])  15.3 us
    ppermute x4, starting transfers between devices, with_halo(): lax.ppermute(head, axis, [((i + 1) % count, i) for i in range(ends)])  13.3 us
    slice x9, local copies, waits for them, and re-layouts, element_terms(): extended[pair_index, member, component, corner_x:corner_x + cells_x, corn...  8.41 us
    dot_general x4, matrix products, element_terms(): jnp.dot(mass_matrix, adjoint_rows, precision=lax.Precision.HIGHEST)  7.02 us
    ppermute x2, waiting for transfers between devices, from_behind(): lax.ppermute(value, axis, [(source, source + steps) for source in range(i...  4.95 us
  transfers between devices with their start and end apart: 10, of which 4 were waited for; matrix products, arithmetic and copies ran while one was open for 3% of the time, Pallas kernels for 0%

commit v1 on v0

--- a/solution.py
+++ b/solution.py
@@ -173,7 +173,8 @@
         partial_volumes = (
             jnp.sum(fields_of, axis=(1, 2)).reshape(len(midpoints), REGIONS, band_cells).sum(axis=2)
         )
-        volumes = lax.psum(partial_volumes, ("gx", "gy"))
+        parts = lax.all_gather(partial_volumes, ("gx", "gy"))
+        volumes = jnp.sum(parts, axis=0)
         position = jnp.zeros((REGIONS,), jnp.int32)
         for depth in range(levels):
             middle = jnp.sqrt(low_end * high_end)

time: 236 us -> 1580 us (6.69)
  waiting for transfers between devices: 20.3 us -> 1460 us
  blocking collectives: 112 us -> 0 us
    all_gather x0 -> x1, waiting for transfers between devices: none -> 1450 us  [bisect_round(): parts = lax.all_gather(partial_volumes, ('gx', 'gy'))]
    psum x1 -> x0, blocking collectives: 112 us -> none  [bisect_round(): volumes = lax.psum(partial_volumes, ('gx', 'gy'))]
  transfers between devices with their start and end apart: 10 -> 11, of which waited for: 4 -> 6; matrix products, arithmetic and copies ran while one was open for 3% -> 0% of each run, Pallas kernels for 0% -> 0%
where the time goes in v1:
time: 1580 us
  waiting for transfers between devices  1460 us (92%)
  local copies, waits for them, and re-layouts  40.1 us (3%)
  starting transfers between devices  34.6 us (2%)
  other arithmetic  17 us (1%)
    all_gather x1, waiting for transfers between devices, bisect_round(): parts = lax.all_gather(partial_volumes, ('gx', 'gy'))  1450 us
  transfers between devices with their start and end apart: 11, of which 6 were waited for; matrix products, arithmetic and copies ran while one was open for 0% of the time, Pallas kernels for 0%

profile of v1, /device:TPU:1, one launch (start us, length us, event | category | flops | bytes accessed | tf_op | source)
XLA Modules:
  0.0 1575.3 jit_solution(17115776771104146260)
XLA Ops:
  7.9 8.8 collective-permute-start
  16.8 1.9 collective-permute-start.1
  19.5 1.2 broadcast_multiply_fusion
  20.7 1.9 collective-permute-start.4
  23.5 1.4 add_minimum_fusion
  25.7 1.3 collective-permute-start.3
  27.0 4.0 collective-permute-start.2
  32.1 1.3 collective-permute-start.5
  35.6 4.2 collective-permute-done.5
  44.6 1.0 pad_slice_fusion.79
  45.6 0.9 pad_slice_fusion.48
  46.5 1.1 stack.30
  47.6 3.7 stack.31
  51.4 1.5 fusion.20
  52.9 1.5 fusion.16
  54.3 3.6 stack.28
  58.0 3.5 stack.29
  61.5 1.5 fusion.19
  63.0 1.5 fusion.15
  64.5 3.7 stack.24
  68.3 3.9 stack.25
  73.9 3.5 stack.26
  77.5 2.8 stack.27
  82.0 1.2 fusion.98
  83.3 1.9 collective-permute-start.7
  85.2 8.5 collective-permute-start.6
  94.6 3.4 collective-permute-start.8
  97.9 1.5 collective-permute-start.9
  99.6 2.8 collective-permute-done.9
  103.1 0.9 fusion.12
  105.1 1450.3 %all-gather.4.cloned.1.call-done = f32[512,63,64]{2,1,0:T(8,128)} async-done(((f32[1,63,64]{2,1,0:T(8,128)}), f32[512,63,64]{2,1,0:T(8,128)}) %all-gather.4.cloned.1.call-update) | async-done | bytes 8257552 | tf_op jit(solution)/shard_map/all_gather | solution.py:176
  1555.4 7.0 reduce_sum.109
  (115 shorter events, 23.2 us)
Async XLA Ops:
  7.2 44.2 %copy-start = (f32[24,24]{1,0:T(8,128)S(1)}, f32[24,24]{1,0:T(8,128)}, u32[]{:S(2)}) copy-start(f32[24,24]{1,0:T(8,128)} %param.14) | copy-start | bytes 6916
  7.2 1548.2 %all-gather.4.cloned.1.call-start = ((), (), s32[]{:S(2)}) async-start(), calls=%async_computation | async-start | bytes 16809984 | tf_op jit(solution)/shard_map/all_gather | solution.py:176
  7.9 15.6 collective-permute-start
  16.8 8.9 collective-permute-start.1
  20.7 11.3 collective-permute-start.4
  25.7 5.4 collective-permute-start.3
  27.0 4.8 collective-permute-start.2
  32.1 7.7 collective-permute-start.5
  45.6 7.3 copy-start.2
  58.0 10.2 copy-start.7
  58.0 10.2 copy-start.8
  58.0 10.2 copy-start.9
  64.5 9.4 copy-start.3
  64.5 9.4 copy-start.4
  73.8 8.1 copy-start.1
  73.9 8.1 copy-start.5
  73.9 8.1 copy-start.6
  73.9 8.1 copy-start.10
  73.9 8.1 copy-start.11
  73.9 8.1 copy-start.13
  81.1 18.4 %copy-start.14 = (f32[63,64]{0,1:T(8,128)S(1)}, f32[63,64]{0,1:T(8,128)}, u32[]{:S(2)}) copy-start(f32[63,64]{0,1:T(8,128)} %constant.25.clone.1) | copy-start | bytes 48388
  82.0 21.1 %copy-start.15 = (f32[8,8,128]{2,1,0:T(8,128)S(1)}, f32[8,8,128]{2,1,0:T(8,128)}, u32[]{:S(2)}) copy-start(f32[8,8,128]{2,1,0:T(8,128)} %get-tuple-element.207) | copy-start | bytes 98308
  82.0 21.1 %copy-start.16 = (f32[8,8,128]{2,1,0:T(8,128)S(1)}, f32[8,8,128]{2,1,0:T(8,128)}, u32[]{:S(2)}) copy-start(f32[8,8,128]{2,1,0:T(8,128)} %get-tuple-element.208) | copy-start | bytes 98308
  83.3 10.5 collective-permute-start.7
  85.2 9.3 collective-permute-start.6
  94.6 5.0 collective-permute-start.8
  97.9 4.4 collective-permute-start.9
  103.1 1464.7 %copy-start.12 = (f32[8,8,128]{2,1,0:T(8,128)}, f32[8,8,128]{2,1,0:T(8,128)S(1)}, u32[]{:S(2)}) copy-start(f32[8,8,128]{2,1,0:T(8,128)S(1)} %get-tuple-element.6) | copy-start | bytes 98308
  105.1 1458.2 %copy-start.17 = (f32[64]{0:T(128)S(1)}, f32[64]{0:T(128)}, u32[]{:S(2)}) copy-start(f32[64]{0:T(128)} %param.15) | copy-start | bytes 772
Sparse Core Ops, SparseCore 0:
  105.1 1450.2 all-gather.3
